TPU v7x, 256 devices: a whole 4x4x8 slice. The times are simulated.
256 devices in a mesh: req: 32 (over x, z), kv: 8 (over y, core).
Axes of the slice: x: 4, y: 4, z: 8, core: 2. Of those that a mesh axis runs over, the one named last changes fastest.
Arguments:
- states: bfloat16 [256, 2560], P(('req', 'kv')), may hold values from -6 to 6
- norm_gain: bfloat16 [2560], replicated, may hold values from 0.099609375 to 1.8984375
- w_query: bfloat16 [2560, 2560], P(None, 'kv'), may hold values from -0.125 to 0.125
- key_projection_weight: bfloat16 [2560, 640], P(None, 'kv'), may hold values from -0.125 to 0.125
- value_projection_weight: bfloat16 [2560, 640], P(None, 'kv'), may hold values from -0.125 to 0.125
- cache_keys: bfloat16 [256, 8, 80, 4096], P('req', 'kv')
- value_cache_slots: bfloat16 [256, 8, 80, 4096], P('req', 'kv'), may hold values from -6 to 6
- lengths: int32 [256], P('req'), may hold values from 1 to 16383, as said below
- write_pos: int32 [256], P('req'), may hold values from 0 to 4095, as said below
- dealing: int32 [256], replicated, may hold values from 0 to 255, each once
Outputs:
- context: bfloat16 [256, 2560], P(('req', 'kv'))
Inputs may be any that keep to these rules, and one draw needn't show every extreme that they name: `lengths`: largest value is reached by some request in every draw. write_pos equals lengths modulo 4096. `dealing`: A permutation of the requests.
All inputs are finite; a program needn't handle non-finite values.
Results may differ from a plain program's by a relative error of at most 0.022.
The roundings to bfloat16 on the way count: a program that leaves them out, or rounds other values in their place, can miss the bound.
Values may be sent and summed in bfloat16 or wider, within the bound.
No kernel may reach another device: no remote copies, remote signals or barrier semaphores. Data moves between devices by JAX's collectives and lax.ppermute only.
A program may use at most 64 MiB of HBM per device.

v0:
```python
import jax
import jax.numpy as jnp
from jax import lax
from jax.sharding import PartitionSpec as P

HEAD_DIMENSION = 80


def apply_rotary(tensor, positions):
    half_width = tensor.shape[-1] // 2
    frequency = 10000.0 ** (-(jnp.arange(half_width, dtype=jnp.float32) * 2.0 / tensor.shape[-1]))
    angles = positions.astype(jnp.float32)[:, None] * frequency[None, :]
    cosine = jnp.cos(angles)[:, None, :]
    sine_part = jnp.sin(angles)[:, None, :]
    front_half = tensor[..., :half_width]
    back_half = tensor[..., half_width:]
    return jnp.concatenate(
        [front_half * cosine - back_half * sine_part, back_half * cosine + front_half * sine_part],
        axis=-1,
    )


def local(
    states,
    norm_gain,
    w_query,
    key_projection_weight,
    value_projection_weight,
    cache_keys,
    value_cache_slots,
    lengths,
    write_pos,
    dealing,
):
    kv_count = lax.axis_size("kv")
    per_device = states.shape[0]
    group_rows = per_device * kv_count
    group_index = lax.axis_index("req")
    kv_index = lax.axis_index("kv")
    req_count = lax.axis_size("req")
    dealt_ids = lax.dynamic_slice_in_dim(dealing, group_index * group_rows, group_rows)
    column_rows = lax.all_gather(states, "req", axis=0, tiled=True)
    column_ids = jnp.arange(req_count, dtype=jnp.int32) * kv_count + kv_index
    pick_in = (dealt_ids[:, None] == column_ids[None, :]).astype(jnp.bfloat16)
    own_part = jnp.dot(pick_in, column_rows, preferred_element_type=jnp.float32).astype(
        jnp.bfloat16
    )
    dealt_rows = lax.psum(own_part, "kv")
    wide_rows = dealt_rows.astype(jnp.float32)
    inv_rms = lax.rsqrt(jnp.mean(wide_rows * wide_rows, axis=1, keepdims=True) + 1e-05)
    normalized_input = (wide_rows * inv_rms * norm_gain.astype(jnp.float32)[None, :]).astype(
        jnp.bfloat16
    )
    head_size = HEAD_DIMENSION
    heads_dev = key_projection_weight.shape[1] // head_size
    queries_per_group = w_query.shape[1] // key_projection_weight.shape[1]
    window_size = cache_keys.shape[3]
    query_vectors = jnp.dot(normalized_input, w_query, preferred_element_type=jnp.float32).reshape(
        group_rows, heads_dev * queries_per_group, head_size
    )
    query_vectors = (
        apply_rotary(query_vectors, lengths)
        .astype(jnp.bfloat16)
        .reshape(group_rows, heads_dev, queries_per_group, head_size)
    )
    fresh_key_rows = jnp.dot(
        normalized_input, key_projection_weight, preferred_element_type=jnp.float32
    ).reshape(group_rows, heads_dev, head_size)
    fresh_key_rows = apply_rotary(fresh_key_rows, lengths).astype(jnp.bfloat16)
    fresh_value_rows = (
        jnp.dot(normalized_input, value_projection_weight, preferred_element_type=jnp.float32)
        .astype(jnp.bfloat16)
        .reshape(group_rows, heads_dev, head_size)
    )
    score_scale = 1.0 / head_size**0.5
    scores = (
        jnp.einsum("rkgh,rkhw->rkgw", query_vectors, cache_keys, preferred_element_type=jnp.float32)
        * score_scale
    )
    own_score = (
        jnp.einsum(
            "rkgh,rkh->rkg", query_vectors, fresh_key_rows, preferred_element_type=jnp.float32
        )
        * score_scale
    )
    slot_ids = lax.broadcasted_iota(jnp.int32, (group_rows, 1, 1, window_size), 3)
    at_write = slot_ids == write_pos[:, None, None, None]
    scores = jnp.where(at_write, own_score[..., None], scores)
    scores = jnp.where(slot_ids <= lengths[:, None, None, None], scores, -jnp.inf)
    row_max = jnp.max(scores, axis=-1, keepdims=True)
    expd = jnp.exp(scores - row_max)
    softmax_weights = (expd / jnp.sum(expd, axis=-1, keepdims=True)).astype(jnp.bfloat16)
    stale_weights = jnp.where(at_write, jnp.zeros((), jnp.bfloat16), softmax_weights)
    fresh_weight = jnp.sum(
        jnp.where(at_write, softmax_weights, jnp.zeros((), jnp.bfloat16)).astype(jnp.float32),
        axis=-1,
    )
    mixed = jnp.einsum(
        "rkgw,rkhw->rkgh", stale_weights, value_cache_slots, preferred_element_type=jnp.float32
    )
    mixed = mixed + fresh_weight[..., None] * fresh_value_rows[:, :, None, :].astype(jnp.float32)
    attended = mixed.reshape(group_rows, heads_dev * queries_per_group * head_size).astype(
        jnp.bfloat16
    )
    group_context = lax.all_gather(attended, "kv", axis=1, tiled=True)
    pick_out = (column_ids[:, None] == dealt_ids[None, :]).astype(jnp.bfloat16)
    routed = jnp.dot(pick_out, group_context, preferred_element_type=jnp.float32).astype(
        jnp.bfloat16
    )
    result = lax.psum_scatter(routed, "req", scatter_dimension=0, tiled=True)
    return result


def solution(mesh):
    in_specs = (
        P(("req", "kv"), None),
        P(),
        P(None, "kv"),
        P(None, "kv"),
        P(None, "kv"),
        P("req", "kv", None, None),
        P("req", "kv", None, None),
        P("req"),
        P("req"),
        P(),
    )
    out_specs = P(("req", "kv"), None)
    return jax.shard_map(local, mesh=mesh, in_specs=in_specs, out_specs=out_specs, check_vma=False)
```

profile of v0, /device:TPU:8, one launch (start us, length us, event | category | flops | bytes accessed | tf_op | source)
XLA Modules:
  0.0 262.5 jit_solution(17877185251697256283)
XLA Ops:
  6.5 0.0 copy-start
  6.5 0.0 all-reduce.3.cloned.1.call-start
  6.6 0.8 convert_element_type.54
  7.3 0.7 iota_compare_fusion
  8.1 0.7 convert_element_type.52
  8.8 0.7 iota_compare_fusion.1
  9.5 52.7 %all-gather = bf16[32,1,2560]{2,1,0:T(2,128)(2,1)S(1)} all-gather(bf16[1,1,2560]{2,1,0:T(2,128)(2,1)} %bitcast.43), channel_id=1, replica_groups=mesh['req'=32,'kv'=8] {'req'}, dimensions={0}, use_global_device_ids=true | all-gather | bytes 168960 | tf_op jit(solution)/shard_map/all_gather | solution.py:42
  62.3 0.8 dynamic_slice.3
  63.0 0.2 convolution_convert_fusion.1
  63.2 21.0 %psum.7 = bf16[8,2560]{1,0:T(8,128)(2,1)S(1)} all-reduce(bf16[8,2560]{1,0:T(8,128)(2,1)S(1)} %convolution_convert_fusion.1), channel_id=1, replica_groups=mesh['req'=32,'kv'=8] {'kv'}, use_global_device_ids=true, to_apply=%region_0.0 | all-reduce | flops 20480 | bytes 81920 | tf_op jit(solution)/shard_map/psum | solution.py:48
  84.2 0.1 fusion.28
  84.4 0.1 multiply_cosine_fusion.1
  84.5 1.3 convolution_bitcast_fusion
  85.7 0.1 fusion.48
  85.9 1.3 fusion.22
  87.1 0.0 copy-done
  87.1 0.5 fusion.52
  87.7 0.1 reshape.241
  87.7 0.1 maximum_bitcast_fusion
  87.8 0.1 subtract_convert_fusion
  87.9 0.2 fusion.43
  88.1 0.0 copy-start.1
  88.1 3.7 %fusion.54 = (f32[8,4]{1,0:T(8,128)S(1)}, f32[8,4,4096]{2,1,0:T(4,128)S(1)}) fusion(bf16[8,1,80,4096]{3,2,1,0:T(8,128)(2,1)} %param.15, f32[8,4]{1,0:T(8,128)S(1)} %broadcast_multiply_fusion, pred[8,4096]{1,0:T(8,128)(4,1)S(1)} %iota_compare_fusion, pred[8,4096]{1,0:T(8,128)(4,1)S(1)} %iota_compare_fusion.1, bf16[8,4,40]{2,1,0:T(4,128)(2,1)S(1)} %get-tuple-element.8, ...), kind=kOutput, calls=%fused_computation.64 | convolution fusion | flops 21641216 | bytes 5838080 | tf_op jit(solution)/shard_map/sub | solution.py:91
  91.8 0.4 convert_reduce_fusion
  92.2 4.0 %fusion.19 = bf16[8,4,80]{2,1,0:T(4,128)(2,1)S(1)} fusion(bf16[8,1,80,4096]{3,2,1,0:T(8,128)(2,1)} %param.16, bf16[8,4,4096]{2,1,0:T(4,128)(2,1)S(1)} %get-tuple-element.6, pred[8,4096]{1,0:T(8,128)(4,1)S(1)} %iota_compare_fusion.1, f32[8,80]{1,0:T(8,128)S(1)} %fusion.22, f32[8,4]{1,0:T(8,128)S(1)} %get-tuple-element.5), kind=kOutput, calls=%fused_computation.13 | convolution fusion | flops 21110272 | bytes 5545600 | tf_op jit(solution)/shard_map/rkgw,rkhw->rkgh/dot_general | solution.py:98
  96.1 0.1 convert_element_type.60
  96.2 13.1 %all-gather.1 = bf16[8,320,8]{1,2,0:T(8,128)(2,1)S(1)} all-gather(bf16[1,320,8]{1,2,0:T(8,128)(2,1)S(1)} %bitcast.42), channel_id=1, replica_groups=mesh['req'=32,'kv'=8] {'kv'}, dimensions={0}, use_global_device_ids=true | all-gather | bytes 46080 | tf_op jit(solution)/shard_map/all_gather | solution.py:105
  109.4 0.1 reshape.248
  109.5 0.9 convolution_convert_fusion
  110.4 0.0 all-reduce.3.cloned.1.call-update
  110.4 0.0 copy-done.1
  110.4 0.7 dynamic-slice
  111.1 142.5 %all-reduce.3.cloned.1.call-done = bf16[32,2560]{1,0:T(8,128)(2,1)} async-done(((bf16[32,2560]{1,0:T(8,128)(2,1)}), bf16[32,2560]{1,0:T(8,128)(2,1)}) %all-reduce.3.cloned.1.call-update) | async-done | bytes 163856
  253.6 2.1 constant_dynamic-slice_fusion
  (5 shorter events, 0.0 us)
Async XLA Ops:
  6.5 80.6 %copy-start = (bf16[2560,320]{0,1:T(8,128)(2,1)S(1)}, bf16[2560,320]{0,1:T(8,128)(2,1)}, u32[]{:S(2)}) copy-start(bf16[2560,320]{0,1:T(8,128)(2,1)} %param.12) | copy-start | bytes 4915204
  6.5 247.0 %all-reduce.3.cloned.1.call-start = ((), (), s32[]{:S(2)}) async-start(), calls=%async_computation | async-start | bytes 327680
  88.1 22.3 %copy-start.1 = (u32[256]{0:T(256)S(1)}, u32[256]{0:T(256)}, u32[]{:S(2)}) copy-start(u32[256]{0:T(256)} %constant.44) | copy-start | bytes 3076
Sparse Core Ops, SparseCore 0:
  110.5 142.9 all-reduce.2
where the time goes:
time: 263 us; the launch traced here: 262 us
  waiting for transfers between devices  143 us (54%)
  blocking collectives  86.9 us (33%)
  between operations  13.5 us (5%)
  matrix products  12 us (5%)
  other arithmetic  3.91 us (1%)
  local copies, waits for them, and re-layouts  3.79 us (1%)
    unnamed x2, waiting for transfers between devices  143 us
    all_gather x1, blocking collectives, local(): column_rows = lax.all_gather(states, 'req', axis=0, tiled=True)  52.7 us
    psum x1, blocking collectives, local(): dealt_rows = lax.psum(own_part, 'kv')  21 us
    all_gather x1, blocking collectives, local(): group_context = lax.all_gather(attended, 'kv', axis=1, tiled=True)  13.1 us
  transfers between devices with their start and end apart: 1, of which 1 were waited for; matrix products, arithmetic and copies ran while one was open for 0% of the time, Pallas kernels for 0%

commit v1 on v0

--- a/solution.py
+++ b/solution.py
@@ -102,7 +102,9 @@
     attended = mixed.reshape(group_rows, heads_dev * queries_per_group * head_size).astype(
         jnp.bfloat16
     )
-    group_context = lax.all_gather(attended, "kv", axis=1, tiled=True)
+    group_context = jnp.concatenate(
+        lax.all_to_all(jnp.stack([attended] * lax.axis_size("kv")), "kv", 0, 0), axis=1
+    )
     pick_out = (column_ids[:, None] == dealt_ids[None, :]).astype(jnp.bfloat16)
     routed = jnp.dot(pick_out, group_context, preferred_element_type=jnp.float32).astype(
         jnp.bfloat16

time: 263 us -> 258 us (0.981)
  blocking collectives: 86.9 us -> 83.7 us
  waiting for transfers between devices: 143 us -> 140 us
    all_gather x1 -> x0, blocking collectives: 13.1 us -> none  [local(): group_context = lax.all_gather(attended, 'kv', axis=1, tiled=True)]
    all_to_all x0 -> x1, blocking collectives: none -> 9.96 us  [local(): lax.all_to_all(jnp.stack([attended] * lax.axis_size('kv')), 'kv', 0, 0)]
where the time goes in v1:
time: 258 us; the launch traced here: 257 us
  waiting for transfers between devices  140 us (54%)
  blocking collectives  83.7 us (32%)
  between operations  13.5 us (5%)
  matrix products  12 us (5%)
  other arithmetic  3.91 us (2%)
  local copies, waits for them, and re-layouts  3.8 us (1%)
    unnamed x2, waiting for transfers between devices  140 us
    all_gather x1, blocking collectives, local(): column_rows = lax.all_gather(states, 'req', axis=0, tiled=True)  52.7 us
    psum x1, blocking collectives, local(): dealt_rows = lax.psum(own_part, 'kv')  21 us
    all_to_all x1, blocking collectives, local(): lax.all_to_all(jnp.stack([attended] * lax.axis_size('kv')), 'kv', 0, 0)  9.96 us
  transfers between devices with their start and end apart: 1, of which 1 were waited for; matrix products, arithmetic and copies ran while one was open for 0% of the time, Pallas kernels for 0%

profile of v1, /device:TPU:8, one launch (start us, length us, event | category | flops | bytes accessed | tf_op | source)
XLA Modules:
  0.0 257.2 jit_solution(11078923148430858313)
XLA Ops:
  6.5 0.0 copy-start
  6.5 0.0 all-reduce.3.cloned.1.call-start
  6.6 0.8 convert_element_type.56
  7.3 0.7 iota_compare_fusion
  8.1 0.7 convert_element_type.54
  8.8 0.7 iota_compare_fusion.1
  9.5 52.7 %all-gather = bf16[32,1,2560]{2,1,0:T(2,128)(2,1)S(1)} all-gather(bf16[1,1,2560]{2,1,0:T(2,128)(2,1)} %bitcast.39), channel_id=1, replica_groups=mesh['req'=32,'kv'=8] {'req'}, dimensions={0}, use_global_device_ids=true | all-gather | bytes 168960 | tf_op jit(solution)/shard_map/all_gather | solution.py:42
  62.3 0.8 dynamic_slice.3
  63.0 0.2 convolution_convert_fusion.1
  63.2 21.0 %psum.7 = bf16[8,2560]{1,0:T(8,128)(2,1)S(1)} all-reduce(bf16[8,2560]{1,0:T(8,128)(2,1)S(1)} %convolution_convert_fusion.1), channel_id=1, replica_groups=mesh['req'=32,'kv'=8] {'kv'}, use_global_device_ids=true, to_apply=%region_0.0 | all-reduce | flops 20480 | bytes 81920 | tf_op jit(solution)/shard_map/psum | solution.py:48
  84.2 0.1 fusion.28
  84.4 0.1 multiply_cosine_fusion.1
  84.5 1.3 convolution_bitcast_fusion
  85.7 0.1 fusion.48
  85.9 1.3 fusion.22
  87.1 0.0 copy-done
  87.1 0.5 fusion.52
  87.7 0.1 reshape.250
  87.7 0.1 maximum_bitcast_fusion
  87.8 0.1 subtract_convert_fusion
  87.9 0.2 fusion.43
  88.1 0.0 copy-start.1
  88.1 3.7 %fusion.54 = (f32[8,4]{1,0:T(8,128)S(1)}, f32[8,4,4096]{2,1,0:T(4,128)S(1)}) fusion(bf16[8,1,80,4096]{3,2,1,0:T(8,128)(2,1)} %param.15, f32[8,4]{1,0:T(8,128)S(1)} %broadcast_multiply_fusion, pred[8,4096]{1,0:T(8,128)(4,1)S(1)} %iota_compare_fusion, pred[8,4096]{1,0:T(8,128)(4,1)S(1)} %iota_compare_fusion.1, bf16[8,4,40]{2,1,0:T(4,128)(2,1)S(1)} %get-tuple-element.8, ...), kind=kOutput, calls=%fused_computation.64 | convolution fusion | flops 21641216 | bytes 5838080 | tf_op jit(solution)/shard_map/sub | solution.py:91
  91.8 0.4 convert_reduce_fusion
  92.2 4.0 %fusion.19 = bf16[8,4,80]{2,1,0:T(4,128)(2,1)S(1)} fusion(bf16[8,1,80,4096]{3,2,1,0:T(8,128)(2,1)} %param.16, bf16[8,4,4096]{2,1,0:T(4,128)(2,1)S(1)} %get-tuple-element.6, pred[8,4096]{1,0:T(8,128)(4,1)S(1)} %iota_compare_fusion.1, f32[8,80]{1,0:T(8,128)S(1)} %fusion.22, f32[8,4]{1,0:T(8,128)S(1)} %get-tuple-element.5), kind=kOutput, calls=%fused_computation.13 | convolution fusion | flops 21110272 | bytes 5545600 | tf_op jit(solution)/shard_map/rkgw,rkhw->rkgh/dot_general | solution.py:98
  96.1 0.1 convert_element_type.62
  96.2 10.0 %all_to_all.5 = bf16[8,8,320]{2,1,0:T(8,128)(2,1)S(1)} all-to-all(bf16[8,8,320]{2,1,0:T(8,128)(2,1)S(1)} %stack.2), channel_id=1, replica_groups=mesh['req'=32,'kv'=8] {'kv'}, dimensions={0} | all-to-all | bytes 81920 | tf_op jit(solution)/shard_map/all_to_all | solution.py:106
  106.2 0.1 reshape.255
  106.3 0.9 convolution_convert_fusion
  107.2 0.0 all-reduce.3.cloned.1.call-update
  107.3 0.0 copy-done.1
  107.3 0.7 dynamic-slice
  107.9 140.4 %all-reduce.3.cloned.1.call-done = bf16[32,2560]{1,0:T(8,128)(2,1)} async-done(((bf16[32,2560]{1,0:T(8,128)(2,1)}), bf16[32,2560]{1,0:T(8,128)(2,1)}) %all-reduce.3.cloned.1.call-update) | async-done | bytes 163856
  248.3 2.1 constant_dynamic-slice_fusion
  (6 shorter events, 0.1 us)
Async XLA Ops:
  6.5 80.6 %copy-start = (bf16[2560,320]{0,1:T(8,128)(2,1)S(1)}, bf16[2560,320]{0,1:T(8,128)(2,1)}, u32[]{:S(2)}) copy-start(bf16[2560,320]{0,1:T(8,128)(2,1)} %param.12) | copy-start | bytes 4915204
  6.5 241.7 %all-reduce.3.cloned.1.call-start = ((), (), s32[]{:S(2)}) async-start(), calls=%async_computation.1 | async-start | bytes 327680
  88.1 19.1 %copy-start.1 = (u32[256]{0:T(256)S(1)}, u32[256]{0:T(256)}, u32[]{:S(2)}) copy-start(u32[256]{0:T(256)} %constant.44) | copy-start | bytes 3076
Sparse Core Ops, SparseCore 0:
  107.4 140.8 all-reduce.2

commit v2 on v0

--- a/solution.py
+++ b/solution.py
@@ -45,7 +45,7 @@
     own_part = jnp.dot(pick_in, column_rows, preferred_element_type=jnp.float32).astype(
         jnp.bfloat16
     )
-    dealt_rows = lax.psum(own_part, "kv")
+    dealt_rows = jnp.sum(lax.all_gather(own_part, "kv"), axis=0)
     wide_rows = dealt_rows.astype(jnp.float32)
     inv_rms = lax.rsqrt(jnp.mean(wide_rows * wide_rows, axis=1, keepdims=True) + 1e-05)
     normalized_input = (wide_rows * inv_rms * norm_gain.astype(jnp.float32)[None, :]).astype(

time: 263 us -> 253 us (0.962)
  blocking collectives: 86.9 us -> 78.7 us
    psum x1 -> x0, blocking collectives: 21 us -> none  [local(): dealt_rows = lax.psum(own_part, 'kv')]
    all_gather x0 -> x1, blocking collectives: none -> 13.1 us  [local(): dealt_rows = jnp.sum(lax.all_gather(own_part, 'kv'), axis=0)]
where the time goes in v2:
time: 253 us
  waiting for transfers between devices  141 us (56%)
  blocking collectives  78.7 us (31%)
  between operations  13.5 us (5%)
  matrix products  12 us (5%)
  other arithmetic  3.96 us (2%)
  local copies, waits for them, and re-layouts  3.79 us (1%)
    unnamed x2, waiting for transfers between devices  141 us
    all_gather x1, blocking collectives, local(): column_rows = lax.all_gather(states, 'req', axis=0, tiled=True)  52.7 us
    all_gather x1, blocking collectives, local(): dealt_rows = jnp.sum(lax.all_gather(own_part, 'kv'), axis=0)  13.1 us
    all_gather x1, blocking collectives, local(): group_context = lax.all_gather(attended, 'kv', axis=1, tiled=True)  12.8 us
  transfers between devices with their start and end apart: 1, of which 1 were waited for; matrix products, arithmetic and copies ran while one was open for 0% of the time, Pallas kernels for 0%

profile of v2, /device:TPU:8, one launch (start us, length us, event | category | flops | bytes accessed | tf_op | source)
XLA Modules:
  0.0 252.9 jit_solution(8552446818918485788)
XLA Ops:
  6.5 0.0 copy-start
  6.5 0.0 all-reduce.3.cloned.1.call-start
  6.6 0.8 convert_element_type.56
  7.3 0.7 iota_compare_fusion
  8.1 0.7 convert_element_type.54
  8.8 0.7 iota_compare_fusion.1
  9.5 52.7 %all-gather.1 = bf16[32,1,2560]{2,1,0:T(2,128)(2,1)S(1)} all-gather(bf16[1,1,2560]{2,1,0:T(2,128)(2,1)} %bitcast.45), channel_id=1, replica_groups=mesh['req'=32,'kv'=8] {'req'}, dimensions={0}, use_global_device_ids=true | all-gather | bytes 168960 | tf_op jit(solution)/shard_map/all_gather | solution.py:42
  62.3 0.8 dynamic_slice.3
  63.0 0.2 convolution_convert_fusion.1
  63.2 13.1 %all-gather = bf16[64,2560]{1,0:T(8,128)(2,1)S(1)} all-gather(bf16[8,2560]{1,0:T(8,128)(2,1)S(1)} %convolution_convert_fusion.1), channel_id=2, replica_groups=mesh['req'=32,'kv'=8] {'kv'}, dimensions={0}, use_global_device_ids=true | all-gather | bytes 368640 | tf_op jit(solution)/shard_map/all_gather | solution.py:48
  76.4 0.1 fusion.28
  76.5 0.1 multiply_cosine_fusion.1
  76.6 1.3 convolution_bitcast_fusion
  77.9 0.1 fusion.48
  78.0 1.3 fusion.22
  79.3 0.0 copy-done
  79.3 0.5 fusion.52
  79.8 0.1 reshape.241
  79.9 0.1 maximum_bitcast_fusion
  80.0 0.1 subtract_convert_fusion
  80.1 0.2 fusion.43
  80.3 0.0 copy-start.1
  80.3 3.7 %fusion.54 = (f32[8,4]{1,0:T(8,128)S(1)}, f32[8,4,4096]{2,1,0:T(4,128)S(1)}) fusion(bf16[8,1,80,4096]{3,2,1,0:T(8,128)(2,1)} %param.15, f32[8,4]{1,0:T(8,128)S(1)} %broadcast_multiply_fusion, pred[8,4096]{1,0:T(8,128)(4,1)S(1)} %iota_compare_fusion, pred[8,4096]{1,0:T(8,128)(4,1)S(1)} %iota_compare_fusion.1, bf16[8,4,40]{2,1,0:T(4,128)(2,1)S(1)} %get-tuple-element.8, ...), kind=kOutput, calls=%fused_computation.65 | convolution fusion | flops 21641216 | bytes 5838080 | tf_op jit(solution)/shard_map/sub | solution.py:91
  84.0 0.4 convert_reduce_fusion
  84.4 4.0 %fusion.19 = bf16[8,4,80]{2,1,0:T(4,128)(2,1)S(1)} fusion(bf16[8,1,80,4096]{3,2,1,0:T(8,128)(2,1)} %param.16, bf16[8,4,4096]{2,1,0:T(4,128)(2,1)S(1)} %get-tuple-element.6, pred[8,4096]{1,0:T(8,128)(4,1)S(1)} %iota_compare_fusion.1, f32[8,80]{1,0:T(8,128)S(1)} %fusion.22, f32[8,4]{1,0:T(8,128)S(1)} %get-tuple-element.5), kind=kOutput, calls=%fused_computation.13 | convolution fusion | flops 21110272 | bytes 5545600 | tf_op jit(solution)/shard_map/rkgw,rkhw->rkgh/dot_general | solution.py:98
  88.3 0.1 convert_element_type.62
  88.4 12.8 %all-gather.2 = bf16[8,320,8]{1,2,0:T(8,128)(2,1)S(1)} all-gather(bf16[1,320,8]{1,2,0:T(8,128)(2,1)S(1)} %bitcast.44), channel_id=1, replica_groups=mesh['req'=32,'kv'=8] {'kv'}, dimensions={0}, use_global_device_ids=true | all-gather | bytes 46080 | tf_op jit(solution)/shard_map/all_gather | solution.py:105
  101.2 0.1 reshape.249
  101.3 0.9 convolution_convert_fusion
  102.2 0.0 all-reduce.3.cloned.1.call-update
  102.2 0.0 copy-done.1
  102.3 0.7 dynamic-slice
  102.9 141.1 %all-reduce.3.cloned.1.call-done = bf16[32,2560]{1,0:T(8,128)(2,1)} async-done(((bf16[32,2560]{1,0:T(8,128)(2,1)}), bf16[32,2560]{1,0:T(8,128)(2,1)}) %all-reduce.3.cloned.1.call-update) | async-done | bytes 163856
  244.0 2.1 constant_dynamic-slice_fusion
  (6 shorter events, 0.1 us)
Async XLA Ops:
  6.5 72.8 %copy-start = (bf16[2560,320]{0,1:T(8,128)(2,1)S(1)}, bf16[2560,320]{0,1:T(8,128)(2,1)}, u32[]{:S(2)}) copy-start(bf16[2560,320]{0,1:T(8,128)(2,1)} %param.12) | copy-start | bytes 4915204
  6.5 237.5 %all-reduce.3.cloned.1.call-start = ((), (), s32[]{:S(2)}) async-start(), calls=%async_computation | async-start | bytes 327680
  80.3 21.9 %copy-start.1 = (u32[256]{0:T(256)S(1)}, u32[256]{0:T(256)}, u32[]{:S(2)}) copy-start(u32[256]{0:T(256)} %constant.45) | copy-start | bytes 3076
Sparse Core Ops, SparseCore 0:
  102.4 141.6 all-reduce.2
